TPU v7x, 256 devices: a whole 4x4x8 slice. The times are simulated.
256 devices in a mesh: seq: 64 (over x, y_hi, z), head: 4 (over y_lo, core).
Axes of the slice: x: 4, y: 4 (y_hi: 2, y_lo: 2; y = y_hi * 2 + y_lo), z: 8, core: 2. Of those that a mesh axis runs over, the one named last changes fastest.
Arguments:
- tokens: bfloat16 [16384, 1024], P('seq'), may hold values from -6 to 6
- queries: bfloat16 [16384, 1024], P('seq', 'head'), may hold values from -8 to 8
- key_rows: bfloat16 [16384, 1024], P('seq', 'head'), may hold values from -8 to 8
- values: bfloat16 [16384, 1024], P('seq', 'head'), may hold values from -6 to 6
- ssm_input: bfloat16 [16384, 2048], P('seq', 'head'), may hold values from -6 to 6
- write_proj: bfloat16 [16384, 128], P('seq'), may hold values from -6 to 6
- read_proj: bfloat16 [16384, 128], P('seq'), may hold values from -6 to 6
- log_decay: float32 [32, 16384], P('head', 'seq'), may hold values from -1 to 0
- attn_project: bfloat16 [1024, 1024], P('head'), may hold values from -0.1875 to 0.1875
- ssm_project: bfloat16 [2048, 1024], P('head'), may hold values from -0.125 to 0.125
- gauss_project: bfloat16 [1024, 768], replicated, may hold values from -0.1875 to 0.1875
- tile_owner: int32 [16384], P('seq'), may hold values from 0 to 3, as said below
Outputs:
- block_out: bfloat16 [16384, 1024], P(('seq', 'head'))
- tile_rows: bfloat16 [64, 4, 4, 32, 768], P('seq', 'head')
Inputs may be any that keep to these rules, and one draw needn't show every extreme that they name: `tile_owner`: in each aligned group of 64 tokens no owner is named by more than 32 tokens; in every block of 256 tokens one owner is named by exactly 32 tokens of each of its groups.
All inputs are finite; a program needn't handle non-finite values.
Results may differ from a plain program's by a relative error of at most 0.023.
Values may be sent and summed in bfloat16 or wider, within the bound.
No kernel may reach another device: no remote copies, remote signals or barrier semaphores. Data moves between devices by JAX's collectives and lax.ppermute only.
A program may use at most 128 MiB of HBM per device.

v0:
```python
import math
import jax
import jax.numpy as jnp
from jax import lax
from jax.sharding import PartitionSpec as P

HDIM = 64


def entering_2(array, axis, combine, identity):
    devices, mine = (lax.axis_size(axis), lax.axis_index(axis))
    everything = jax.tree.map(
        lambda part, kind: lax.all_gather(part.astype(kind), axis),
        array,
        (jnp.bfloat16, jnp.bfloat16),
    )
    start = jax.tree.map(
        lambda part, zero: jnp.broadcast_to(jnp.asarray(zero, part.dtype), part.shape),
        array,
        identity,
    )

    def hop(k, before):
        reached = k < mine
        new = combine(
            before, jax.tree.map(lambda part, own: part[k].astype(own.dtype), everything, array)
        )
        return jax.tree.map(lambda a, b: jnp.where(reached, a, b), new, before)

    return lax.fori_loop(0, devices, hop, start)


def chain_pieces(ssm_input, write_proj, read_proj, log_decay):
    row_count = write_proj.shape[0]
    head_count = log_decay.shape[0]
    head_width = ssm_input.shape[1] // head_count
    cumulative = jnp.cumsum(log_decay, axis=1)
    inputs_heads = ssm_input.reshape(row_count, head_count, head_width)
    later_rows = lax.broadcasted_iota(jnp.int32, (row_count, row_count), 0)
    earlier_cols = lax.broadcasted_iota(jnp.int32, (row_count, row_count), 1)
    log_gaps = cumulative[:, :, None] - cumulative[:, None, :]
    decays = jnp.exp(jnp.where((later_rows >= earlier_cols)[None], log_gaps, -jnp.inf))
    cross_terms = jnp.dot(read_proj, write_proj.T, preferred_element_type=jnp.float32)
    mixing = (decays * cross_terms[None]).astype(jnp.bfloat16)
    inner_part = jnp.einsum(
        "hts,shp->thp", mixing, inputs_heads, preferred_element_type=jnp.float32
    )
    tail_decay = jnp.exp(cumulative[:, -1:] - cumulative)
    tail_inputs = (inputs_heads.astype(jnp.float32) * tail_decay.T[:, :, None]).astype(jnp.bfloat16)
    local_state = jnp.einsum(
        "sn,shp->hnp", write_proj, tail_inputs, preferred_element_type=jnp.float32
    )
    total_decay = jnp.exp(cumulative[:, -1])
    return (cumulative, inner_part, local_state, total_decay)


def chain_output(cumulative, inner_part, entering, read_proj):
    entering_low = entering.astype(jnp.bfloat16)
    outer_part = jnp.einsum(
        "tn,hnp->thp", read_proj, entering_low, preferred_element_type=jnp.float32
    )
    mixture = inner_part + outer_part * jnp.exp(cumulative).T[:, :, None]
    scaled = mixture * lax.rsqrt(jnp.mean(mixture * mixture, axis=2, keepdims=True) + 1e-05)
    return scaled.reshape(scaled.shape[0], -1).astype(jnp.bfloat16)


def combine_states(earlier, latter):
    decay_first, state_first = earlier
    decay_second, state_second = latter
    return (decay_first * decay_second, decay_second[:, None, None] * state_first + state_second)


def pass_states(local_state, total_decay):
    identity = (jnp.ones_like(total_decay), jnp.zeros_like(local_state))
    prefix = entering_2((total_decay, local_state), "seq", combine_states, identity)
    return prefix[1]


def fold_keys(query_heads, key_rows, values):
    row_count, head_count, head_width = query_heads.shape
    scale = 1.0 / math.sqrt(head_width)
    initial = (
        jnp.full((head_count, row_count), -jnp.inf, jnp.float32),
        jnp.zeros((head_count, row_count), jnp.float32),
        jnp.zeros((head_count, row_count, head_width), jnp.float32),
    )
    key_piece = lax.all_gather(key_rows, "seq", axis=0, tiled=True)
    value_piece = lax.all_gather(values, "seq", axis=0, tiled=True)
    piece_rows = key_piece.shape[0]
    block_rows = math.gcd(piece_rows, 1024)

    def one_step(block_index, carry_state):
        run_max, run_sum, accumulated = carry_state
        key_block = lax.dynamic_slice_in_dim(
            key_piece, block_index * block_rows, block_rows, 0
        ).reshape(block_rows, head_count, head_width)
        value_block = lax.dynamic_slice_in_dim(
            value_piece, block_index * block_rows, block_rows, 0
        ).reshape(block_rows, head_count, head_width)
        scores = (
            jnp.einsum("qhd,khd->hqk", query_heads, key_block, preferred_element_type=jnp.float32)
            * scale
        )
        new_max = jnp.maximum(run_max, jnp.max(scores, axis=2))
        shrink = jnp.exp(run_max - new_max)
        raised = jnp.exp(scores - new_max[:, :, None])
        run_sum = run_sum * shrink + jnp.sum(raised, axis=2)
        accumulated = accumulated * shrink[:, :, None] + jnp.einsum(
            "hqk,khd->hqd",
            raised.astype(jnp.bfloat16),
            value_block,
            preferred_element_type=jnp.float32,
        )
        return (new_max, run_sum, accumulated)

    run_max, run_sum, accumulated = lax.fori_loop(0, piece_rows // block_rows, one_step, initial)
    attended = accumulated / run_sum[:, :, None]
    return (
        attended.transpose(1, 0, 2).reshape(row_count, head_count * head_width).astype(jnp.bfloat16)
    )


def slot_rank(owners_here, owner_count, group_rows):
    row_count = owners_here.shape[0]
    one_hot = (owners_here[:, None] == jnp.arange(owner_count, dtype=jnp.int32)[None, :]).astype(
        jnp.bfloat16
    )
    later_rows = lax.broadcasted_iota(jnp.int32, (row_count, row_count), 0)
    earlier_cols = lax.broadcasted_iota(jnp.int32, (row_count, row_count), 1)
    before = (
        (earlier_cols < later_rows) & (later_rows // group_rows == earlier_cols // group_rows)
    ).astype(jnp.bfloat16)
    counted = jnp.dot(before, one_hot, preferred_element_type=jnp.float32)
    return jnp.sum(counted * one_hot.astype(jnp.float32), axis=1)


def per_device(
    tokens,
    queries,
    key_rows,
    values,
    ssm_input,
    write_proj,
    read_proj,
    log_decay,
    attn_project,
    ssm_project,
    gauss_project,
    tile_owner,
):
    row_count = queries.shape[0]
    head_count = queries.shape[1] // HDIM
    query_heads = queries.reshape(row_count, head_count, HDIM)
    attended = fold_keys(query_heads, key_rows, values)
    cumulative, inner_part, local_state, total_decay = chain_pieces(
        ssm_input, write_proj, read_proj, log_decay
    )
    entering = pass_states(local_state, total_decay)
    ssm_mix = chain_output(cumulative, inner_part, entering, read_proj)
    owner_count = lax.axis_size("head")
    own_index = lax.axis_index("head")
    sub_rows = row_count // owner_count
    capacity = sub_rows // 2
    width_out = gauss_project.shape[1]
    slot_count = owner_count * capacity
    slot_ids = jnp.arange(slot_count, dtype=jnp.float32)
    update = lax.psum_scatter(
        (
            jnp.dot(attended, attn_project, preferred_element_type=jnp.float32)
            + jnp.dot(ssm_mix, ssm_project, preferred_element_type=jnp.float32)
        ).astype(jnp.bfloat16),
        "head",
        scatter_dimension=0,
        tiled=True,
    ).astype(jnp.float32)
    own_tokens = lax.dynamic_slice_in_dim(tokens, own_index * sub_rows, sub_rows, 0)
    block_out = (own_tokens.astype(jnp.float32) + update).astype(jnp.bfloat16)
    gaussians = jnp.dot(block_out, gauss_project, preferred_element_type=jnp.float32).astype(
        jnp.bfloat16
    )
    owners_here = lax.dynamic_slice_in_dim(tile_owner, own_index * sub_rows, sub_rows, 0)
    slot_value = owners_here.astype(jnp.float32) * capacity + slot_rank(
        owners_here, owner_count, sub_rows
    )
    selector = (slot_ids[:, None] == slot_value[None, :]).astype(jnp.bfloat16)
    packed = jnp.dot(selector, gaussians, preferred_element_type=jnp.float32).astype(jnp.bfloat16)
    packed = packed.reshape(owner_count, capacity, width_out)
    received = lax.all_to_all(packed, "head", split_axis=0, concat_axis=0, tiled=True)
    tile_rows = received.reshape(1, 1, owner_count, capacity, width_out)
    return (block_out, tile_rows)


def solution(mesh):
    in_specs = (
        P("seq", None),
        P("seq", "head"),
        P("seq", "head"),
        P("seq", "head"),
        P("seq", "head"),
        P("seq", None),
        P("seq", None),
        P("head", "seq"),
        P("head", None),
        P("head", None),
        P(),
        P("seq"),
    )
    out_specs = (P(("seq", "head"), None), P("seq", "head", None, None, None))
    return jax.shard_map(
        per_device, mesh=mesh, in_specs=in_specs, out_specs=out_specs, check_vma=False
    )
```

profile of v0, /device:TPU:1, one launch (start us, length us, event | category | flops | bytes accessed | tf_op | source)
XLA Modules:
  0.0 632.4 jit_solution(15385614962645540333)
XLA Ops:
  18.4 161.7 %all-reduce = bf16[512]{0:T(512)(128)(2,1)S(1)} all-reduce(bf16[512]{0:T(512)(128)(2,1)S(1)} %dynamic-update-slice), channel_id=2, replica_groups=mesh['seq'=64,'head'=4] {'seq'}, use_global_device_ids=true, to_apply=%add | all-reduce | flops 512 | bytes 2048
  182.3 82.8 %while.33 = (s32[]{:T(128)}, f32[8,128,64]{2,1,0:T(8,128)S(1)}, s32[]{:T(128)}, bf16[64,8]{1,0:T(8,128)(2,1)S(1)}, bf16[64,8,128,64]{2,3,1,0:T(8,128)(2,1)}, /*index=5*/s32[]{:T(128)}, s32[]{:T(128)}) while((s32[]{:T(128)}, f32[8,128,64]{2,1,0:T(8,128)S(1)}, s32[]{:T(128)}, bf16[64,8]{1,0:T(8,128)(2,1)S(1)}, ...), condition=%wide.region_7.8_spmd.clone, body=%wide.region_6.7_spmd.clone.sunk | while | flops 327692 | bytes 1179833 | solution.py:30
  267.7 41.6 %all-gather.6.cloned.1.call-done = bf16[16384,256]{0,1:T(8,128)(2,1)} async-done(((bf16[256,256]{0,1:T(8,128)(2,1)}), bf16[16384,256]{0,1:T(8,128)(2,1)}) %all-gather.6.cloned.1.call-update) | async-done | bytes 8388624 | tf_op jit(solution)/shard_map/all_gather | solution.py:87
  309.3 148.9 %all-gather.8.cloned.1.call-done = bf16[16384,256]{0,1:T(8,128)(2,1)} async-done(((bf16[256,256]{0,1:T(8,128)(2,1)}), bf16[16384,256]{0,1:T(8,128)(2,1)}) %all-gather.8.cloned.1.call-update) | async-done | bytes 8388624 | tf_op jit(solution)/shard_map/all_gather | solution.py:88
  458.2 133.3 %while.32 = (s32[]{:T(128)}, f32[4,256]{1,0:T(4,128)S(1)}, f32[4,256]{1,0:T(4,128)S(1)}, f32[4,256,64]{1,2,0:T(8,128)S(1)}, bf16[16384,256]{0,1:T(8,128)(2,1)}, ...) while((s32[]{:T(128)}, f32[4,256]{1,0:T(4,128)S(1)}, ...), condition=%wide.region_3.0_spmd.clone, body=%wide.region_0.0_spmd.clone.sunk | while | flops 277025792 | bytes 33226948 | solution.py:116
  459.5 2.7 bitcast_reduce_fusion.2
  462.2 3.0 fusion.66
  467.8 2.7 bitcast_reduce_fusion.2
  470.5 3.0 fusion.66
  476.1 2.7 bitcast_reduce_fusion.2
  478.8 3.0 fusion.66
  484.5 2.7 bitcast_reduce_fusion.2
  487.2 3.0 fusion.66
  495.5 3.0 fusion.66
  503.8 3.0 fusion.66
  512.2 3.0 fusion.66
  520.5 3.0 fusion.66
  528.8 3.0 fusion.66
  534.4 2.7 bitcast_reduce_fusion.2
  537.1 3.0 fusion.66
  542.8 2.7 bitcast_reduce_fusion.2
  545.5 3.0 fusion.66
  551.1 2.7 bitcast_reduce_fusion.2
  553.8 3.0 fusion.66
  559.4 2.7 bitcast_reduce_fusion.2
  562.1 3.0 fusion.66
  567.8 2.7 bitcast_reduce_fusion.2
  570.5 3.0 fusion.66
  578.8 3.0 fusion.66
  587.1 3.0 fusion.66
  595.9 20.9 %reduce-scatter.2.cloned.1.call-done = bf16[64,1024]{1,0:T(8,128)(2,1)} async-done(((bf16[256,1024]{1,0:T(8,128)(2,1)}), bf16[64,1024]{1,0:T(8,128)(2,1)}) %reduce-scatter.2.cloned.1.call-update) | async-done | bytes 131088 | tf_op jit(solution)/shard_map/reduce_scatter | solution.py:167
  618.4 6.8 %all_to_all.5 = bf16[4,32,768]{2,1,0:T(8,128)(2,1)S(1)} all-to-all(bf16[4,32,768]{2,1,0:T(8,128)(2,1)S(1)} %bitcast.92), channel_id=1, replica_groups=mesh['seq'=64,'head'=4] {'head'}, dimensions={0} | all-to-all | bytes 393216 | tf_op jit(solution)/shard_map/all_to_all | solution.py:188
  (432 shorter events, 162.0 us)
Async XLA Ops:
  7.2 610.6 %copy-start = (bf16[1024,768]{1,0:T(8,128)(2,1)S(1)}, bf16[1024,768]{1,0:T(8,128)(2,1)}, u32[]{:S(2)}) copy-start(bf16[1024,768]{1,0:T(8,128)(2,1)} %param.26) | copy-start | bytes 4718596
  7.2 175.1 %all-gather.10.cloned.1.call-start = ((), (), s32[]{:S(2)}) async-start(), calls=%async_computation.5 | async-start | bytes 8519680 | tf_op jit(solution)/shard_map/all_gather | solution.py:13
  12.0 297.3 %all-gather.6.cloned.1.call-start = ((), (), s32[]{:S(2)}) async-start(), calls=%async_computation.2 | async-start | bytes 8519680 | tf_op jit(solution)/shard_map/all_gather | solution.py:87
  13.7 444.4 %all-gather.8.cloned.1.call-start = ((), (), s32[]{:S(2)}) async-start(), calls=%async_computation.3 | async-start | bytes 8519680 | tf_op jit(solution)/shard_map/all_gather | solution.py:88
  15.5 601.3 %reduce-scatter.2.cloned.1.call-start = ((), (), s32[]{:S(2)}) async-start(), calls=%async_computation.4 | async-start | bytes 655360 | tf_op jit(solution)/shard_map/reduce_scatter | solution.py:167
  182.3 82.8 %copy-start.4 = (bf16[256,128]{1,0:T(8,128)(2,1)S(1)}, bf16[256,128]{1,0:T(8,128)(2,1)}, u32[]{:S(2)}) copy-start(bf16[256,128]{1,0:T(8,128)(2,1)} %param.22) | copy-start | bytes 196612
  458.2 136.1 %copy-start.2 = (bf16[256,1024]{1,0:T(8,128)(2,1)S(1)}, bf16[256,1024]{1,0:T(8,128)(2,1)}, u32[]{:S(2)}) copy-start(bf16[256,1024]{1,0:T(8,128)(2,1)} %param.24) | copy-start | bytes 1572868
  462.2 3.4 copy-start.1
  470.5 3.4 copy-start.1
  478.8 3.4 copy-start.1
  487.2 3.4 copy-start.1
  495.5 3.4 copy-start.1
  503.8 3.4 copy-start.1
  512.2 3.4 copy-start.1
  520.5 3.4 copy-start.1
  528.8 3.4 copy-start.1
  537.1 3.4 copy-start.1
  545.5 3.4 copy-start.1
  553.8 3.4 copy-start.1
  562.1 3.4 copy-start.1
  570.5 3.4 copy-start.1
  578.8 3.4 copy-start.1
  587.1 3.4 copy-start.1
  591.5 4.0 copy-start.5
  617.8 8.1 %copy-start.3 = (bf16[64,1024]{1,0:T(8,128)(2,1)}, bf16[64,1024]{1,0:T(8,128)(2,1)S(1)}, u32[]{:S(2)}) copy-start(bf16[64,1024]{1,0:T(8,128)(2,1)S(1)} %add_convert_fusion) | copy-start | bytes 393220
Sparse Core Ops, SparseCore 0:
  12.2 148.4 all-gather.9
  164.8 144.4 all-gather.5
  312.7 145.3 all-gather.7
  595.6 21.1 reduce-scatter.1
where the time goes:
time: 634 us; the launch traced here: 632 us
  waiting for transfers between devices  211 us (33%)
  blocking collectives  168 us (26%)
  local copies, waits for them, and re-layouts  105 us (17%)
  matrix products  66 us (10%)
  other arithmetic  63.3 us (10%)
  between operations  14.5 us (2%)
    unnamed x1, blocking collectives  162 us
    all_gather x1, waiting for transfers between devices, fold_keys(): value_piece = lax.all_gather(values, 'seq', axis=0, tiled=True)  149 us
    dynamic_slice x128, local copies, waits for them, and re-layouts, hop(): part[k].astype(own.dtype)  70.3 us
    reduce_sum x16, other arithmetic, one_step(): run_sum = run_sum * shrink + jnp.sum(raised, axis=2)  48.5 us
    dot_general x16, matrix products, one_step(): jnp.einsum('qhd,khd->hqk', query_heads, key_block, preferred_element_type...  43.1 us
    all_gather x1, waiting for transfers between devices, fold_keys(): key_piece = lax.all_gather(key_rows, 'seq', axis=0, tiled=True)  41.6 us
    reduce_scatter x1, waiting for transfers between devices, per_device(): lax.psum_scatter((jnp.dot(attended, attn_project, preferred_element_type=...  20.9 us
    dynamic_slice x16, local copies, waits for them, and re-layouts, one_step(): lax.dynamic_slice_in_dim(value_piece, block_index * block_rows, block_row...  20.5 us
  transfers between devices with their start and end apart: 4, of which 3 were waited for; matrix products, arithmetic and copies ran while one was open for 14% of the time, Pallas kernels for 0%

commit v1 on v0

--- a/solution.py
+++ b/solution.py
@@ -85,7 +85,9 @@
         jnp.zeros((head_count, row_count, head_width), jnp.float32),
     )
     key_piece = lax.all_gather(key_rows, "seq", axis=0, tiled=True)
-    value_piece = lax.all_gather(values, "seq", axis=0, tiled=True)
+    value_piece = jnp.concatenate(
+        lax.all_to_all(jnp.stack([values] * lax.axis_size("seq")), "seq", 0, 0), axis=0
+    )
     piece_rows = key_piece.shape[0]
     block_rows = math.gcd(piece_rows, 1024)
 

time: 634 us -> 739 us (1.17)
  blocking collectives: 168 us -> 368 us
  waiting for transfers between devices: 211 us -> 40.9 us
  matrix products: 66 us -> 101 us
  local copies, waits for them, and re-layouts: 105 us -> 129 us
  starting transfers between devices: 0.16 us -> 15.6 us
    unnamed x1, blocking collectives: 162 us -> 362 us
    all_gather x1 -> x0, waiting for transfers between devices: 149 us -> none  [fold_keys(): value_piece = lax.all_gather(values, 'seq', axis=0, tiled=True)]
    all_gather x1, waiting for transfers between devices: 41.6 us -> 0.01 us  [fold_keys(): key_piece = lax.all_gather(key_rows, 'seq', axis=0, tiled=True)]
    dot_general x16, matrix products: 13.9 us -> 48.6 us  [one_step(): jnp.einsum('hqk,khd->hqd', raised.astype(jnp.bfloat16), value_block, pref...]
    reduce_scatter x1, waiting for transfers between devices: 20.9 us -> 40.8 us  [per_device(): lax.psum_scatter((jnp.dot(attended, attn_project, preferred_element_type=...]
    dynamic_slice x0 -> x16, local copies, waits for them, and re-layouts: none -> 17.3 us  [one_step(): lax.dynamic_slice_in_dim(key_piece, block_index * block_rows, block_rows, 0)]
    all_to_all x0 -> x1, starting transfers between devices: none -> 15.5 us  [fold_keys(): lax.all_to_all(jnp.stack([values] * lax.axis_size('seq')), 'seq', 0, 0)]
    all_to_all x0 -> x1, local copies, waits for them, and re-layouts: none -> 11.9 us  [fold_keys(): lax.all_to_all(jnp.stack([values] * lax.axis_size('seq')), 'seq', 0, 0)]
  transfers between devices with their start and end apart: 4 -> 4, of which waited for: 3 -> 1; matrix products, arithmetic and copies ran while one was open for 14% -> 14% of each run, Pallas kernels for 0% -> 0%
where the time goes in v1:
time: 739 us; the launch traced here: 734 us
  blocking collectives  368 us (50%)
  local copies, waits for them, and re-layouts  129 us (17%)
  matrix products  101 us (14%)
  other arithmetic  60.9 us (8%)
  waiting for transfers between devices  40.9 us (6%)
  starting transfers between devices  15.6 us (2%)
  between operations  14.6 us (2%)
    unnamed x1, blocking collectives  362 us
    dynamic_slice x128, local copies, waits for them, and re-layouts, hop(): part[k].astype(own.dtype)  70.1 us
    dot_general x16, matrix products, one_step(): jnp.einsum('hqk,khd->hqd', raised.astype(jnp.bfloat16), value_block, pref...  48.6 us
    reduce_sum x16, other arithmetic, one_step(): run_sum = run_sum * shrink + jnp.sum(raised, axis=2)  46.1 us
    dot_general x16, matrix products, one_step(): jnp.einsum('qhd,khd->hqk', query_heads, key_block, preferred_element_type...  43.1 us
    reduce_scatter x1, waiting for transfers between devices, per_device(): lax.psum_scatter((jnp.dot(attended, attn_project, preferred_element_type=...  40.8 us
    dynamic_slice x32, local copies, waits for them, and re-layouts, one_step(): lax.dynamic_slice_in_dim(value_piece, block_index * block_rows, block_row...  20.6 us
    dynamic_slice x16, local copies, waits for them, and re-layouts, one_step(): lax.dynamic_slice_in_dim(key_piece, block_index * block_rows, block_rows, 0)  17.3 us
  transfers between devices with their start and end apart: 4, of which 1 were waited for; matrix products, arithmetic and copies ran while one was open for 14% of the time, Pallas kernels for 0%

profile of v1, /device:TPU:1, one launch (start us, length us, event | category | flops | bytes accessed | tf_op | source)
XLA Modules:
  0.0 734.0 jit_solution(1324960553260437137)
XLA Ops:
  13.0 4.2 stack.2
  17.2 15.5 %all-to-all-start = ((bf16[64,256,256]{1,2,0:T(8,128)(2,1)}), bf16[64,256,256]{1,2,0:T(8,128)(2,1)}, u32[]{:S(2)}, u32[]{:S(2)}) async-start(bf16[64,256,256]{1,2,0:T(8,128)(2,1)} %stack.2), calls=%async_computation | async-start | bytes 16777216 | tf_op jit(solution)/shard_map/all_to_all | solution.py:89
  35.4 361.6 %all-reduce = bf16[512]{0:T(512)(128)(2,1)S(1)} all-reduce(bf16[512]{0:T(512)(128)(2,1)S(1)} %dynamic-update-slice), channel_id=2, replica_groups=mesh['seq'=64,'head'=4] {'seq'}, use_global_device_ids=true, to_apply=%add | all-reduce | flops 512 | bytes 2048
  398.0 11.9 %copy.51 = bf16[64,256,256]{2,1,0:T(8,128)(2,1)} copy(bf16[64,256,256]{1,2,0:T(8,128)(2,1)} %all-to-all-done) | data formatting | bytes 16777216 | tf_op jit(solution)/shard_map/all_to_all | solution.py:89
  409.9 82.6 %while.33 = (s32[]{:T(128)}, f32[8,128,64]{2,1,0:T(8,128)S(1)}, s32[]{:T(128)}, bf16[64,8]{1,0:T(8,128)(2,1)S(1)}, bf16[64,8,128,64]{2,3,1,0:T(8,128)(2,1)}, /*index=5*/s32[]{:T(128)}, s32[]{:T(128)}) while((s32[]{:T(128)}, f32[8,128,64]{2,1,0:T(8,128)S(1)}, s32[]{:T(128)}, bf16[64,8]{1,0:T(8,128)(2,1)S(1)}, ...), condition=%wide.region_7.8_spmd.clone, body=%wide.region_6.7_spmd.clone.sunk | while | flops 327692 | bytes 1179833 | solution.py:30
  495.1 177.0 %while.32 = (s32[]{:T(128)}, f32[4,256]{1,0:T(4,128)S(1)}, f32[4,256]{1,0:T(4,128)S(1)}, f32[4,256,64]{1,2,0:T(8,128)S(1)}, bf16[16384,256]{0,1:T(8,128)(2,1)}, ...) while((s32[]{:T(128)}, f32[4,256]{1,0:T(4,128)S(1)}, ...), condition=%wide.region_3.0_spmd.clone, body=%wide.region_0.0_spmd.clone.sunk | while | flops 277025792 | bytes 17498288 | solution.py:118
  498.9 2.9 fusion.66
  503.1 3.0 fusion.68
  510.0 2.9 fusion.66
  514.2 3.0 fusion.68
  521.1 2.9 fusion.66
  525.3 3.0 fusion.68
  532.1 2.9 fusion.66
  536.3 3.0 fusion.68
  543.2 2.9 fusion.66
  547.4 3.0 fusion.68
  558.5 3.0 fusion.68
  569.5 3.0 fusion.68
  576.4 2.9 fusion.66
  580.6 3.0 fusion.68
  587.5 2.9 fusion.66
  591.7 3.0 fusion.68
  602.7 3.0 fusion.68
  613.8 3.0 fusion.68
  624.9 3.0 fusion.68
  635.9 3.0 fusion.68
  647.0 3.0 fusion.68
  653.9 2.9 fusion.66
  658.1 3.0 fusion.68
  669.1 3.0 fusion.68
  677.6 40.8 %reduce-scatter.2.cloned.1.call-done = bf16[64,1024]{1,0:T(8,128)(2,1)} async-done(((bf16[256,1024]{1,0:T(8,128)(2,1)}), bf16[64,1024]{1,0:T(8,128)(2,1)}) %reduce-scatter.2.cloned.1.call-update) | async-done | bytes 131088 | tf_op jit(solution)/shard_map/reduce_scatter | solution.py:169
  720.1 6.7 all_to_all.10
  (439 shorter events, 203.5 us)
Async XLA Ops:
  7.2 712.3 %copy-start = (bf16[1024,768]{1,0:T(8,128)(2,1)S(1)}, bf16[1024,768]{1,0:T(8,128)(2,1)}, u32[]{:S(2)}) copy-start(bf16[1024,768]{1,0:T(8,128)(2,1)} %param.26) | copy-start | bytes 4718596
  7.2 402.7 %all-gather.7.cloned.1.call-start = ((), (), s32[]{:S(2)}) async-start(), calls=%async_computation.5 | async-start | bytes 8519680 | tf_op jit(solution)/shard_map/all_gather | solution.py:13
  17.2 15.6 %copy-start.4 = (bf16[256,256]{1,0:T(8,128)(2,1)S(1)}, bf16[256,256]{1,0:T(8,128)(2,1)}, u32[]{:S(2)}) copy-start(bf16[256,256]{1,0:T(8,128)(2,1)} %param.18) | copy-start | bytes 393220
  17.2 16.5 %copy-start.7 = (u32[256]{0:T(256)S(1)}, u32[256]{0:T(256)}, u32[]{:S(2)}) copy-start(u32[256]{0:T(256)} %constant.128) | copy-start | bytes 3076
  17.2 379.8 %copy-start.5 = (bf16[256,256]{1,0:T(8,128)(2,1)S(1)}, bf16[256,256]{1,0:T(8,128)(2,1)}, u32[]{:S(2)}) copy-start(bf16[256,256]{1,0:T(8,128)(2,1)} %param.17) | copy-start | bytes 393220
  17.2 380.6 %copy-start.2 = (bf16[256,128]{1,0:T(8,128)(2,1)S(1)}, bf16[256,128]{1,0:T(8,128)(2,1)}, u32[]{:S(2)}) copy-start(bf16[256,128]{1,0:T(8,128)(2,1)} %param.21) | copy-start | bytes 196612
  17.2 380.6 %copy-start.3 = (bf16[256,128]{1,0:T(8,128)(2,1)S(1)}, bf16[256,128]{1,0:T(8,128)(2,1)}, u32[]{:S(2)}) copy-start(bf16[256,128]{1,0:T(8,128)(2,1)} %param.22) | copy-start | bytes 196612
  17.2 380.8 %all-to-all-start = ((bf16[64,256,256]{1,2,0:T(8,128)(2,1)}), bf16[64,256,256]{1,2,0:T(8,128)(2,1)}, u32[]{:S(2)}, u32[]{:S(2)}) async-start(bf16[64,256,256]{1,2,0:T(8,128)(2,1)} %stack.2), calls=%async_computation | async-start | bytes 16777216 | tf_op jit(solution)/shard_map/all_to_all | solution.py:89
  32.8 462.4 %all-gather.5.cloned.1.call-start = ((), (), s32[]{:S(2)}) async-start(), calls=%async_computation.3 | async-start | bytes 8519680 | tf_op jit(solution)/shard_map/all_gather | solution.py:87
  33.6 684.8 %reduce-scatter.2.cloned.1.call-start = ((), (), s32[]{:S(2)}) async-start(), calls=%async_computation.4 | async-start | bytes 655360 | tf_op jit(solution)/shard_map/reduce_scatter | solution.py:169
  672.2 5.0 copy-start.6
  719.4 8.0 %copy-start.1 = (bf16[64,1024]{1,0:T(8,128)(2,1)}, bf16[64,1024]{1,0:T(8,128)(2,1)S(1)}, u32[]{:S(2)}) copy-start(bf16[64,1024]{1,0:T(8,128)(2,1)S(1)} %add_convert_fusion) | copy-start | bytes 393220
Sparse Core Ops, SparseCore 0:
  12.2 240.0 all-gather.6
  256.4 145.6 all-gather.4
  677.3 41.0 reduce-scatter.1
